TPU v7x, 32 devices: a whole 2x2x4 slice. The times are simulated.
32 devices in a mesh: slab: 8 (over y, x, core), view: 4 (over z).
Axes of the slice: x: 2, y: 2, z: 4, core: 2. Of those that a mesh axis runs over, the one named last changes fastest.
Arguments:
- estimate: float32 [4, 1024, 1024], P(None, 'slab'), may hold values from 0.5 to 2
- views: float32 [4, 4, 1024, 1024], P('view', None, 'slab'), may hold values from 0.25 to 4
- psf: float32 [4, 1024, 1024], P('view', 'slab'), as said below
- pattern_mult: int32 [4, 8], P('view'), may hold values from 0 to 63
- pattern_shift: int32 [4, 8], P('view'), may hold values from 0 to 127
- interp: float32 [4, 8, 128], P('view'), may hold values from 0.05 to 0.45
Outputs:
- updated: float32 [4, 1024, 1024], P(None, 'slab')
Inputs may be any that keep to these rules, and one draw needn't show every extreme that they name: `psf`: every entry is positive.
All inputs are finite; a program needn't handle non-finite values.
Results may differ from a plain program's by a relative error of at most 0.0001.
Values sent between devices are 32-bit elements; how exact they have to be, the bound alone decides.
No kernel may reach another device: no remote copies, remote signals or barrier semaphores. Data moves between devices by JAX's collectives and lax.ppermute only.
A program may use at most 128 MiB of HBM per device.

v0:
```python
import math
import jax
import jax.numpy as jnp
from jax import lax
from jax.sharding import PartitionSpec as P

highest = lax.Precision.HIGHEST


def block_matrix(multiplier, shifting, weights):
    positions = jnp.arange(128, dtype=jnp.int32)
    first_col = ((2 * multiplier[:, None] + 1) * positions[None, :] + shifting[:, None]) % 128
    second_col = (first_col + 1) % 128
    columns = positions[None, None, :]
    lower = (columns == first_col[:, :, None]).astype(jnp.float32)
    upper = (columns == second_col[:, :, None]).astype(jnp.float32)
    return (1.0 - weights)[:, :, None] * lower + weights[:, :, None] * upper


def angle_tables(rows, cols, length):
    row_index = lax.iota(jnp.int32, rows)[:, None]
    col_index = lax.iota(jnp.int32, cols)[None, :]
    angles = (row_index * col_index % length).astype(jnp.float32) * (2.0 * math.pi / length)
    return (jnp.cos(angles), jnp.sin(angles))


def contract(form, real_part, imag_part, cosine, sine_table, direction, want_imag):
    real_cos = jnp.einsum(form, real_part, cosine, precision=highest)
    if imag_part is None:
        return (real_cos, direction * jnp.einsum(form, real_part, sine_table, precision=highest))
    imag_sin = jnp.einsum(form, imag_part, sine_table, precision=highest)
    out_real = real_cos - direction * imag_sin
    if not want_imag:
        return (out_real, None)
    real_sin = jnp.einsum(form, real_part, sine_table, precision=highest)
    imag_cos = jnp.einsum(form, imag_part, cosine, precision=highest)
    return (out_real, imag_cos + direction * real_sin)


def complex_times(real_part, imag_part, cosine, sine_table):
    return (
        real_part * cosine - imag_part * sine_table,
        real_part * sine_table + imag_part * cosine,
    )


def factored(real_part, imag_part, axis, direction, forward, want_imag):
    length = real_part.shape[axis]
    second = 128
    first = length // second
    if axis == 2:
        leading, trailing = ("rx", "")
    else:
        leading, trailing = ("r", "z")
    outer = real_part.shape
    shape = outer[:axis] + (first, second) + outer[axis + 1 :]
    real_part = real_part.reshape(shape)
    if imag_part is not None:
        imag_part = imag_part.reshape(shape)
    first_cos, first_sin = angle_tables(first, first, first)
    second_cos, second_sin = angle_tables(second, second, second)
    twist_cos, twist_sin = angle_tables(first, second, length)
    if axis == 1:
        twist_cos = twist_cos[:, :, None]
        twist_sin = twist_sin[:, :, None]
    twist_sin = direction * twist_sin
    if forward:
        real_part, imag_part = contract(
            leading + "ab" + trailing + ",ak->" + leading + "kb" + trailing,
            real_part,
            imag_part,
            first_cos,
            first_sin,
            direction,
            True,
        )
        real_part, imag_part = complex_times(real_part, imag_part, twist_cos, twist_sin)
        real_part, imag_part = contract(
            leading + "kb" + trailing + ",bm->" + leading + "km" + trailing,
            real_part,
            imag_part,
            second_cos,
            second_sin,
            direction,
            want_imag,
        )
    else:
        real_part, imag_part = contract(
            leading + "km" + trailing + ",mb->" + leading + "kb" + trailing,
            real_part,
            imag_part,
            second_cos,
            second_sin,
            direction,
            True,
        )
        real_part, imag_part = complex_times(real_part, imag_part, twist_cos, twist_sin)
        real_part, imag_part = contract(
            leading + "kb" + trailing + ",ka->" + leading + "ab" + trailing,
            real_part,
            imag_part,
            first_cos,
            first_sin,
            direction,
            want_imag,
        )
    real_part = real_part.reshape(outer)
    if imag_part is not None:
        imag_part = imag_part.reshape(outer)
    return (real_part, imag_part)


def to_columns(real_part, imag_part):
    depth_real, depth_imag = factored(real_part, imag_part, 2, -1.0, True, True)
    moved_real, moved_imag = (
        lax.all_to_all(depth_real, "slab", split_axis=2, concat_axis=1, tiled=True),
        lax.all_to_all(depth_imag, "slab", split_axis=2, concat_axis=1, tiled=True),
    )
    return factored(moved_real, moved_imag, 1, -1.0, True, True)


def to_planes(real_part, imag_part):
    width_real, width_imag = factored(real_part, imag_part, 1, 1.0, False, True)
    moved_real, moved_imag = (
        lax.all_to_all(width_real, "slab", split_axis=1, concat_axis=2, tiled=True),
        lax.all_to_all(width_imag, "slab", split_axis=1, concat_axis=2, tiled=True),
    )
    scaling = 1.0 / (width_real.shape[1] * moved_real.shape[2])
    out_real, out_imag = factored(moved_real, moved_imag, 2, 1.0, False, False)
    return (out_real * scaling, None)


def shards(estimate, views, psf, pattern_mult, pattern_shift, interp):
    row_count, slab_width, depth = estimate.shape
    blocks = block_matrix(pattern_mult[0], pattern_shift[0], interp[0])
    block_count = depth // 128
    shaped = estimate.reshape(row_count, slab_width, block_count, 128)
    sampled = jnp.einsum("bij,yxbj->yxbi", blocks, shaped, precision=highest).reshape(
        row_count, slab_width, depth
    )

    def pack(volume):
        return (volume, None)

    packed_real, packed_imag = pack(sampled)
    packed_real = jnp.concatenate([packed_real, psf], 0)
    spectra_real, spectra_imag = to_columns(packed_real, packed_imag)
    transfer_real = spectra_real[-1:]
    transfer_imag = spectra_imag[-1:]
    spectra_real = spectra_real[:-1]
    spectra_imag = spectra_imag[:-1]
    filtered_real = spectra_real * transfer_real - spectra_imag * transfer_imag
    filtered_imag = spectra_real * transfer_imag + spectra_imag * transfer_real
    blurred_real, blurred_imag = to_planes(filtered_real, filtered_imag)
    quotient = views[0] / blurred_real
    packed_real, packed_imag = pack(quotient)
    spectra_real, spectra_imag = to_columns(packed_real, packed_imag)
    filtered_real = spectra_real * transfer_real + spectra_imag * transfer_imag
    filtered_imag = spectra_imag * transfer_real - spectra_real * transfer_imag
    smeared_real, smeared_imag = to_planes(filtered_real, filtered_imag)
    correction = jnp.einsum(
        "bij,yxbi->yxbj",
        blocks,
        smeared_real.reshape(row_count, slab_width, block_count, 128),
        precision=highest,
    ).reshape(row_count, slab_width, depth)
    log_terms = jnp.log(correction)
    view_count = lax.axis_size("view")
    summed = lax.psum(log_terms, "view")
    return estimate * jnp.exp(summed / view_count)


def solution(mesh):
    placed = (
        P(None, "slab", None),
        P("view", None, "slab", None),
        P("view", "slab", None),
        P("view", None),
        P("view", None),
        P("view", None, None),
    )
    return jax.shard_map(
        shards, mesh=mesh, in_specs=placed, out_specs=P(None, "slab", None), check_vma=False
    )
```

profile of v0, /device:TPU:0, one launch (start us, length us, event | category | flops | bytes accessed | tf_op | source)
XLA Modules:
  0.0 555.8 jit_solution(18437681724977504398)
XLA Ops:
  10.0 3.6 fusion.121
  15.3 3.1 copy.145
  20.8 4.7 subtract_bitcast_fusion.2
  25.5 3.0 fusion.16
  28.6 3.2 multiply_add_fusion.1
  31.8 3.8 copy.157
  35.7 5.2 all-to-all-start.1
  40.8 3.0 fusion.18
  43.9 3.2 multiply_subtract_fusion.1
  47.1 3.6 copy.151
  50.7 39.3 %all-to-all-done.1 = f32[5,128,1024]{1,0,2:T(8,128)} async-done(((f32[5,128,1024]{1,0,2:T(8,128)}), f32[5,128,1024]{1,0,2:T(8,128)}, u32[]{:S(2)}, u32[]{:S(2)}) %all-to-all-start.1) | async-done | bytes 2621472 | tf_op jit(solution)/shard_map/all_to_all | solution.py:117
  90.0 4.8 all-to-all-start
  95.0 3.1 copy.268
  98.1 3.8 fusion
  101.9 3.9 fusion.2
  105.8 37.9 %all-to-all-done = f32[5,128,1024]{1,0,2:T(8,128)} async-done(((f32[5,128,1024]{1,0,2:T(8,128)}), f32[5,128,1024]{1,0,2:T(8,128)}, u32[]{:S(2)}, u32[]{:S(2)}) %all-to-all-start) | async-done | bytes 2621472 | tf_op jit(solution)/shard_map/all_to_all | solution.py:116
  143.7 3.1 copy.265
  146.8 4.3 multiply_add_fusion
  151.1 3.4 subtract_bitcast_fusion.1
  154.6 2.9 fusion.10
  157.4 2.9 fusion.8
  160.3 3.0 subtract_bitcast_fusion
  163.4 3.0 add_bitcast_fusion
  173.7 2.9 fusion.39
  176.7 3.3 fusion.77
  180.0 2.9 subtract_bitcast_fusion.6
  185.9 4.4 all-to-all-start.2
  190.3 4.5 fusion.75
  194.8 3.0 add_bitcast_fusion.6
  198.1 2.7 copy.181
  200.9 16.1 %all-to-all-done.2 = f32[4,1024,128]{2,0,1:T(4,128)} async-done(((f32[4,1024,128]{2,0,1:T(4,128)}), f32[4,1024,128]{2,0,1:T(4,128)}, u32[]{:S(2)}, u32[]{:S(2)}) %all-to-all-start.2) | async-done | bytes 2097184 | tf_op jit(solution)/shard_map/all_to_all | solution.py:125
  217.0 4.5 all-to-all-start.3
  225.1 3.4 fusion.171
  228.4 19.5 %all-to-all-done.3 = f32[4,1024,128]{2,0,1:T(4,128)} async-done(((f32[4,1024,128]{2,0,1:T(4,128)}), f32[4,1024,128]{2,0,1:T(4,128)}, u32[]{:S(2)}, u32[]{:S(2)}) %all-to-all-start.3) | async-done | bytes 2097184 | tf_op jit(solution)/shard_map/all_to_all | solution.py:126
  256.5 3.1 fusion.47
  259.6 3.3 bitcast_divide_fusion
  269.6 3.0 multiply_add_fusion.5
  275.3 4.4 all-to-all-start.5
  279.6 4.0 fusion.69
  286.3 2.7 copy.189
  289.0 17.3 %all-to-all-done.5 = f32[4,128,1024]{1,0,2:T(4,128)} async-done(((f32[4,128,1024]{1,0,2:T(4,128)}), f32[4,128,1024]{1,0,2:T(4,128)}, u32[]{:S(2)}, u32[]{:S(2)}) %all-to-all-start.5) | async-done | bytes 2097184 | tf_op jit(solution)/shard_map/all_to_all | solution.py:117
  306.3 4.5 all-to-all-start.4
  313.1 3.2 fusion.31
  316.3 3.2 fusion.33
  319.5 17.8 %all-to-all-done.4 = f32[4,128,1024]{1,0,2:T(4,128)} async-done(((f32[4,128,1024]{1,0,2:T(4,128)}), f32[4,128,1024]{1,0,2:T(4,128)}, u32[]{:S(2)}, u32[]{:S(2)}) %all-to-all-start.4) | async-done | bytes 2097184 | tf_op jit(solution)/shard_map/all_to_all | solution.py:116
  339.6 3.7 multiply_add_fusion.4
  360.5 2.8 convolution_subtract_fusion.1
  363.3 2.9 fusion.27
  366.2 2.9 fusion.53
  369.1 2.9 subtract_bitcast_fusion.3
  372.4 2.8 copy.214
  375.3 4.4 all-to-all-start.6
  379.6 4.5 fusion.51
  384.1 3.0 add_bitcast_fusion.3
  387.5 2.7 copy.219
  390.2 16.1 %all-to-all-done.6 = f32[4,1024,128]{2,0,1:T(4,128)} async-done(((f32[4,1024,128]{2,0,1:T(4,128)}), f32[4,1024,128]{2,0,1:T(4,128)}, u32[]{:S(2)}, u32[]{:S(2)}) %all-to-all-start.6) | async-done | bytes 2097184 | tf_op jit(solution)/shard_map/all_to_all | solution.py:125
  406.3 4.3 all-to-all-start.7
  412.6 3.4 fusion.167
  416.0 21.3 %all-to-all-done.7 = f32[4,1024,128]{2,0,1:T(4,128)} async-done(((f32[4,1024,128]{2,0,1:T(4,128)}), f32[4,1024,128]{2,0,1:T(4,128)}, u32[]{:S(2)}, u32[]{:S(2)}) %all-to-all-start.7) | async-done | bytes 2097184 | tf_op jit(solution)/shard_map/all_to_all | solution.py:126
  445.8 2.9 fusion.43
  448.7 3.3 multiply_bitcast_fusion
  457.7 84.9 %all-reduce.2.cloned.1.call-done = f32[4,128,1024]{1,2,0:T(8,128)} async-done(((f32[4,128,1024]{1,2,0:T(8,128)}), f32[4,128,1024]{1,2,0:T(8,128)}) %all-reduce.2.cloned.1.call-update) | async-done | bytes 2097168 | tf_op jit(solution)/shard_map/psum | solution.py:169
  542.6 3.2 exponential_multiply_fusion
  545.8 2.9 copy.226
  (76 shorter events, 81.1 us)
Async XLA Ops:
  18.4 2.4 copy-start
  25.5 3.1 copy-start.1
  35.7 54.4 %all-to-all-start.1 = ((f32[5,128,1024]{1,0,2:T(8,128)}), f32[5,128,1024]{1,0,2:T(8,128)}, u32[]{:S(2)}, u32[]{:S(2)}) async-start(f32[5,128,1024]{1,0,2:T(8,128)} %copy.157), calls=%async_computation.1 | async-start | bytes 8388608 | tf_op jit(solution)/shard_map/all_to_all | solution.py:117
  40.8 3.0 copy-start.2
  90.0 53.7 %all-to-all-start = ((f32[5,128,1024]{1,0,2:T(8,128)}), f32[5,128,1024]{1,0,2:T(8,128)}, u32[]{:S(2)}, u32[]{:S(2)}) async-start(f32[5,128,1024]{1,0,2:T(8,128)} %copy.151), calls=%async_computation | async-start | bytes 8388608 | tf_op jit(solution)/shard_map/all_to_all | solution.py:116
  146.8 4.3 copy-start.6
  176.7 3.3 copy-start.4
  185.9 31.0 %all-to-all-start.2 = ((f32[4,1024,128]{2,0,1:T(4,128)}), f32[4,1024,128]{2,0,1:T(4,128)}, u32[]{:S(2)}, u32[]{:S(2)}) async-start(f32[4,1024,128]{2,0,1:T(4,128)} %copy.176), calls=%async_computation.2 | async-start | bytes 4194304 | tf_op jit(solution)/shard_map/all_to_all | solution.py:125
  200.9 20.6 %copy-start.10 = (f32[1,4,128,1024]{3,2,1,0:T(8,128)S(1)}, f32[1,4,128,1024]{3,2,1,0:T(8,128)}, u32[]{:S(2)}) copy-start(f32[1,4,128,1024]{3,2,1,0:T(8,128)} %param.7) | copy-start | bytes 6291460
  217.0 31.0 %all-to-all-start.3 = ((f32[4,1024,128]{2,0,1:T(4,128)}), f32[4,1024,128]{2,0,1:T(4,128)}, u32[]{:S(2)}, u32[]{:S(2)}) async-start(f32[4,1024,128]{2,0,1:T(4,128)} %copy.181), calls=%async_computation.3 | async-start | bytes 4194304 | tf_op jit(solution)/shard_map/all_to_all | solution.py:126
  249.7 2.1 copy-start.7
  256.5 3.1 copy-start.11
  267.1 2.5 copy-start.5
  275.3 31.0 %all-to-all-start.5 = ((f32[4,128,1024]{1,0,2:T(4,128)}), f32[4,128,1024]{1,0,2:T(4,128)}, u32[]{:S(2)}, u32[]{:S(2)}) async-start(f32[4,128,1024]{1,0,2:T(4,128)} %copy.195), calls=%async_computation.5 | async-start | bytes 4194304 | tf_op jit(solution)/shard_map/all_to_all | solution.py:117
  306.3 31.0 %all-to-all-start.4 = ((f32[4,128,1024]{1,0,2:T(4,128)}), f32[4,128,1024]{1,0,2:T(4,128)}, u32[]{:S(2)}, u32[]{:S(2)}) async-start(f32[4,128,1024]{1,0,2:T(4,128)} %copy.189), calls=%async_computation.4 | async-start | bytes 4194304 | tf_op jit(solution)/shard_map/all_to_all | solution.py:116
  339.6 3.7 copy-start.9
  366.2 2.9 copy-start.3
  375.3 31.0 %all-to-all-start.6 = ((f32[4,1024,128]{2,0,1:T(4,128)}), f32[4,1024,128]{2,0,1:T(4,128)}, u32[]{:S(2)}, u32[]{:S(2)}) async-start(f32[4,1024,128]{2,0,1:T(4,128)} %copy.214), calls=%async_computation.6 | async-start | bytes 4194304 | tf_op jit(solution)/shard_map/all_to_all | solution.py:125
  406.3 31.0 %all-to-all-start.7 = ((f32[4,1024,128]{2,0,1:T(4,128)}), f32[4,1024,128]{2,0,1:T(4,128)}, u32[]{:S(2)}, u32[]{:S(2)}) async-start(f32[4,1024,128]{2,0,1:T(4,128)} %copy.219), calls=%async_computation.7 | async-start | bytes 4194304 | tf_op jit(solution)/shard_map/all_to_all | solution.py:126
  410.6 132.0 %all-reduce.2.cloned.1.call-start = ((), (), s32[]{:S(2)}) async-start(), calls=%async_computation.8 | async-start | bytes 4194304 | tf_op jit(solution)/shard_map/psum | solution.py:169
  439.0 2.1 copy-start.8
  448.7 3.3 copy-start.12
Sparse Core Ops, SparseCore 0:
  455.9 86.6 all-reduce.1
where the time goes:
time: 560 us; the launch traced here: 556 us
  waiting for transfers between devices  270 us (48%)
  matrix products  172 us (31%)
  local copies, waits for them, and re-layouts  55.7 us (10%)
  starting transfers between devices  36.6 us (7%)
  between operations  14.4 us (3%)
  other arithmetic  7.07 us (1%)
    psum x1, waiting for transfers between devices, shards(): summed = lax.psum(log_terms, 'view')  84.9 us
    all_to_all x2, waiting for transfers between devices, to_columns(): lax.all_to_all(depth_imag, 'slab', split_axis=2, concat_axis=1, tiled=True)  56.6 us
    all_to_all x2, waiting for transfers between devices, to_columns(): lax.all_to_all(depth_real, 'slab', split_axis=2, concat_axis=1, tiled=True)  55.7 us
    dot_general x16, matrix products, contract(): real_cos = jnp.einsum(form, real_part, cosine, precision=highest)  48.2 us
    dot_general x14, matrix products, contract(): imag_sin = jnp.einsum(form, imag_part, sine_table, precision=highest)  41.1 us
    all_to_all x2, waiting for transfers between devices, to_planes(): lax.all_to_all(width_imag, 'slab', split_axis=1, concat_axis=2, tiled=True)  40.8 us
    dot_general x12, matrix products, contract(): real_sin = jnp.einsum(form, real_part, sine_table, precision=highest)  36.4 us
    dot_general x12, matrix products, contract(): imag_cos = jnp.einsum(form, imag_part, cosine, precision=highest)  35.7 us
  transfers between devices with their start and end apart: 9, of which 9 were waited for; matrix products, arithmetic and copies ran while one was open for 13% of the time, Pallas kernels for 0%

commit v1 on v0

--- a/solution.py
+++ b/solution.py
@@ -166,7 +166,7 @@
     ).reshape(row_count, slab_width, depth)
     log_terms = jnp.log(correction)
     view_count = lax.axis_size("view")
-    summed = lax.psum(log_terms, "view")
+    summed = jnp.sum(lax.all_gather(log_terms, "view"), axis=0)
     return estimate * jnp.exp(summed / view_count)
 
 

time: 560 us -> 633 us (1.13)
  waiting for transfers between devices: 270 us -> 333 us
    all_gather x0 -> x1, waiting for transfers between devices: none -> 148 us  [shards(): summed = jnp.sum(lax.all_gather(log_terms, 'view'), axis=0)]
    psum x1 -> x0, waiting for transfers between devices: 84.9 us -> none  [shards(): summed = lax.psum(log_terms, 'view')]
  transfers between devices with their start and end apart: 9 -> 9, of which waited for: 9 -> 9; matrix products, arithmetic and copies ran while one was open for 13% -> 12% of each run, Pallas kernels for 0% -> 0%
where the time goes in v1:
time: 633 us; the launch traced here: 628 us
  waiting for transfers between devices  333 us (53%)
  matrix products  172 us (27%)
  local copies, waits for them, and re-layouts  59.2 us (9%)
  starting transfers between devices  36.6 us (6%)
  between operations  14.4 us (2%)
  other arithmetic  13 us (2%)
    all_gather x1, waiting for transfers between devices, shards(): summed = jnp.sum(lax.all_gather(log_terms, 'view'), axis=0)  148 us
    all_to_all x2, waiting for transfers between devices, to_columns(): lax.all_to_all(depth_imag, 'slab', split_axis=2, concat_axis=1, tiled=True)  56.6 us
    all_to_all x2, waiting for transfers between devices, to_columns(): lax.all_to_all(depth_real, 'slab', split_axis=2, concat_axis=1, tiled=True)  55.7 us
    dot_general x16, matrix products, contract(): real_cos = jnp.einsum(form, real_part, cosine, precision=highest)  48.2 us
    dot_general x14, matrix products, contract(): imag_sin = jnp.einsum(form, imag_part, sine_table, precision=highest)  41.1 us
    all_to_all x2, waiting for transfers between devices, to_planes(): lax.all_to_all(width_imag, 'slab', split_axis=1, concat_axis=2, tiled=True)  40.8 us
    dot_general x12, matrix products, contract(): real_sin = jnp.einsum(form, real_part, sine_table, precision=highest)  36.4 us
    dot_general x12, matrix products, contract(): imag_cos = jnp.einsum(form, imag_part, cosine, precision=highest)  35.7 us
  transfers between devices with their start and end apart: 9, of which 9 were waited for; matrix products, arithmetic and copies ran while one was open for 12% of the time, Pallas kernels for 0%

profile of v1, /device:TPU:0, one launch (start us, length us, event | category | flops | bytes accessed | tf_op | source)
XLA Modules:
  0.0 628.3 jit_solution(9787072392832856917)
XLA Ops:
  10.0 3.6 fusion.121
  15.3 3.1 copy.143
  20.8 4.7 subtract_bitcast_fusion.2
  25.5 3.0 fusion.16
  28.6 3.2 multiply_add_fusion.1
  31.8 3.8 copy.155
  35.7 5.2 all-to-all-start.1
  40.8 3.0 fusion.18
  43.9 3.2 multiply_subtract_fusion.1
  47.1 3.6 copy.149
  50.7 39.3 %all-to-all-done.1 = f32[5,128,1024]{1,0,2:T(8,128)} async-done(((f32[5,128,1024]{1,0,2:T(8,128)}), f32[5,128,1024]{1,0,2:T(8,128)}, u32[]{:S(2)}, u32[]{:S(2)}) %all-to-all-start.1) | async-done | bytes 2621472 | tf_op jit(solution)/shard_map/all_to_all | solution.py:117
  90.0 4.8 all-to-all-start
  95.0 3.1 copy.268
  98.1 3.8 fusion
  101.9 3.9 fusion.2
  105.8 37.9 %all-to-all-done = f32[5,128,1024]{1,0,2:T(8,128)} async-done(((f32[5,128,1024]{1,0,2:T(8,128)}), f32[5,128,1024]{1,0,2:T(8,128)}, u32[]{:S(2)}, u32[]{:S(2)}) %all-to-all-start) | async-done | bytes 2621472 | tf_op jit(solution)/shard_map/all_to_all | solution.py:116
  143.7 3.1 copy.265
  146.8 4.3 multiply_add_fusion
  151.1 3.4 subtract_bitcast_fusion.1
  154.6 2.9 fusion.10
  157.4 2.9 fusion.8
  160.3 3.0 subtract_bitcast_fusion
  163.4 3.0 add_bitcast_fusion
  173.7 2.9 fusion.39
  176.7 3.3 fusion.77
  180.0 2.9 subtract_bitcast_fusion.6
  185.9 4.4 all-to-all-start.2
  190.3 4.5 fusion.75
  194.8 3.0 add_bitcast_fusion.6
  198.1 2.7 copy.179
  200.9 16.1 %all-to-all-done.2 = f32[4,1024,128]{2,0,1:T(4,128)} async-done(((f32[4,1024,128]{2,0,1:T(4,128)}), f32[4,1024,128]{2,0,1:T(4,128)}, u32[]{:S(2)}, u32[]{:S(2)}) %all-to-all-start.2) | async-done | bytes 2097184 | tf_op jit(solution)/shard_map/all_to_all | solution.py:125
  217.0 4.5 all-to-all-start.3
  225.1 3.4 fusion.171
  228.4 19.5 %all-to-all-done.3 = f32[4,1024,128]{2,0,1:T(4,128)} async-done(((f32[4,1024,128]{2,0,1:T(4,128)}), f32[4,1024,128]{2,0,1:T(4,128)}, u32[]{:S(2)}, u32[]{:S(2)}) %all-to-all-start.3) | async-done | bytes 2097184 | tf_op jit(solution)/shard_map/all_to_all | solution.py:126
  256.5 3.1 fusion.47
  259.6 3.3 bitcast_divide_fusion
  269.6 3.0 multiply_add_fusion.5
  275.3 4.4 all-to-all-start.5
  279.6 4.0 fusion.69
  289.0 17.3 %all-to-all-done.5 = f32[4,128,1024]{1,0,2:T(4,128)} async-done(((f32[4,128,1024]{1,0,2:T(4,128)}), f32[4,128,1024]{1,0,2:T(4,128)}, u32[]{:S(2)}, u32[]{:S(2)}) %all-to-all-start.5) | async-done | bytes 2097184 | tf_op jit(solution)/shard_map/all_to_all | solution.py:117
  306.3 4.5 all-to-all-start.4
  313.1 3.2 fusion.31
  316.3 3.2 fusion.33
  319.5 17.8 %all-to-all-done.4 = f32[4,128,1024]{1,0,2:T(4,128)} async-done(((f32[4,128,1024]{1,0,2:T(4,128)}), f32[4,128,1024]{1,0,2:T(4,128)}, u32[]{:S(2)}, u32[]{:S(2)}) %all-to-all-start.4) | async-done | bytes 2097184 | tf_op jit(solution)/shard_map/all_to_all | solution.py:116
  339.6 3.7 multiply_add_fusion.4
  360.5 2.8 convolution_subtract_fusion.1
  363.3 2.9 fusion.27
  366.2 2.9 fusion.53
  369.1 2.9 subtract_bitcast_fusion.3
  372.4 2.8 copy.212
  375.3 4.4 all-to-all-start.6
  379.6 4.5 fusion.51
  384.1 3.0 add_bitcast_fusion.3
  390.2 16.1 %all-to-all-done.6 = f32[4,1024,128]{2,0,1:T(4,128)} async-done(((f32[4,1024,128]{2,0,1:T(4,128)}), f32[4,1024,128]{2,0,1:T(4,128)}, u32[]{:S(2)}, u32[]{:S(2)}) %all-to-all-start.6) | async-done | bytes 2097184 | tf_op jit(solution)/shard_map/all_to_all | solution.py:125
  406.3 4.3 all-to-all-start.7
  412.6 3.4 fusion.167
  416.0 21.3 %all-to-all-done.7 = f32[4,1024,128]{2,0,1:T(4,128)} async-done(((f32[4,1024,128]{2,0,1:T(4,128)}), f32[4,1024,128]{2,0,1:T(4,128)}, u32[]{:S(2)}, u32[]{:S(2)}) %all-to-all-start.7) | async-done | bytes 2097184 | tf_op jit(solution)/shard_map/all_to_all | solution.py:126
  445.8 2.9 fusion.43
  448.7 3.3 multiply_bitcast_fusion
  458.2 148.1 %all-gather.2.cloned.1.call-done = f32[4,4,128,1024]{3,2,1,0:T(8,128)} async-done(((f32[1,4,128,1024]{3,2,1,0:T(8,128)}), f32[4,4,128,1024]{3,2,1,0:T(8,128)}) %all-gather.2.cloned.1.call-update) | async-done | bytes 8388624 | tf_op jit(solution)/shard_map/all_gather | solution.py:169
  606.3 5.9 reduce_sum.9
  612.2 2.9 copy.287
  615.1 3.2 exponential_multiply_fusion
  618.3 2.9 copy.226
  (79 shorter events, 87.1 us)
Async XLA Ops:
  18.4 2.4 copy-start
  25.5 3.1 copy-start.1
  35.7 54.4 %all-to-all-start.1 = ((f32[5,128,1024]{1,0,2:T(8,128)}), f32[5,128,1024]{1,0,2:T(8,128)}, u32[]{:S(2)}, u32[]{:S(2)}) async-start(f32[5,128,1024]{1,0,2:T(8,128)} %copy.155), calls=%async_computation.1 | async-start | bytes 8388608 | tf_op jit(solution)/shard_map/all_to_all | solution.py:117
  40.8 3.0 copy-start.2
  90.0 53.7 %all-to-all-start = ((f32[5,128,1024]{1,0,2:T(8,128)}), f32[5,128,1024]{1,0,2:T(8,128)}, u32[]{:S(2)}, u32[]{:S(2)}) async-start(f32[5,128,1024]{1,0,2:T(8,128)} %copy.149), calls=%async_computation | async-start | bytes 8388608 | tf_op jit(solution)/shard_map/all_to_all | solution.py:116
  146.8 4.3 copy-start.6
  176.7 3.3 copy-start.4
  185.9 31.0 %all-to-all-start.2 = ((f32[4,1024,128]{2,0,1:T(4,128)}), f32[4,1024,128]{2,0,1:T(4,128)}, u32[]{:S(2)}, u32[]{:S(2)}) async-start(f32[4,1024,128]{2,0,1:T(4,128)} %copy.174), calls=%async_computation.2 | async-start | bytes 4194304 | tf_op jit(solution)/shard_map/all_to_all | solution.py:125
  200.9 20.6 %copy-start.10 = (f32[1,4,128,1024]{3,2,1,0:T(8,128)S(1)}, f32[1,4,128,1024]{3,2,1,0:T(8,128)}, u32[]{:S(2)}) copy-start(f32[1,4,128,1024]{3,2,1,0:T(8,128)} %param.7) | copy-start | bytes 6291460
  217.0 31.0 %all-to-all-start.3 = ((f32[4,1024,128]{2,0,1:T(4,128)}), f32[4,1024,128]{2,0,1:T(4,128)}, u32[]{:S(2)}, u32[]{:S(2)}) async-start(f32[4,1024,128]{2,0,1:T(4,128)} %copy.179), calls=%async_computation.3 | async-start | bytes 4194304 | tf_op jit(solution)/shard_map/all_to_all | solution.py:126
  249.7 2.1 copy-start.7
  256.5 3.1 copy-start.11
  267.1 2.5 copy-start.5
  275.3 31.0 %all-to-all-start.5 = ((f32[4,128,1024]{1,0,2:T(4,128)}), f32[4,128,1024]{1,0,2:T(4,128)}, u32[]{:S(2)}, u32[]{:S(2)}) async-start(f32[4,128,1024]{1,0,2:T(4,128)} %copy.193), calls=%async_computation.5 | async-start | bytes 4194304 | tf_op jit(solution)/shard_map/all_to_all | solution.py:117
  306.3 31.0 %all-to-all-start.4 = ((f32[4,128,1024]{1,0,2:T(4,128)}), f32[4,128,1024]{1,0,2:T(4,128)}, u32[]{:S(2)}, u32[]{:S(2)}) async-start(f32[4,128,1024]{1,0,2:T(4,128)} %copy.187), calls=%async_computation.4 | async-start | bytes 4194304 | tf_op jit(solution)/shard_map/all_to_all | solution.py:116
  339.6 3.7 copy-start.9
  366.2 2.9 copy-start.3
  375.3 31.0 %all-to-all-start.6 = ((f32[4,1024,128]{2,0,1:T(4,128)}), f32[4,1024,128]{2,0,1:T(4,128)}, u32[]{:S(2)}, u32[]{:S(2)}) async-start(f32[4,1024,128]{2,0,1:T(4,128)} %copy.212), calls=%async_computation.6 | async-start | bytes 4194304 | tf_op jit(solution)/shard_map/all_to_all | solution.py:125
  406.3 31.0 %all-to-all-start.7 = ((f32[4,1024,128]{2,0,1:T(4,128)}), f32[4,1024,128]{2,0,1:T(4,128)}, u32[]{:S(2)}, u32[]{:S(2)}) async-start(f32[4,1024,128]{2,0,1:T(4,128)} %copy.217), calls=%async_computation.7 | async-start | bytes 4194304 | tf_op jit(solution)/shard_map/all_to_all | solution.py:126
  410.6 195.7 %all-gather.2.cloned.1.call-start = ((), (), s32[]{:S(2)}) async-start(), calls=%async_computation.8 | async-start | bytes 10485760 | tf_op jit(solution)/shard_map/all_gather | solution.py:169
  439.0 2.1 copy-start.8
  448.7 3.3 copy-start.12
Sparse Core Ops, SparseCore 0:
  456.4 149.8 all-gather.1
